TPU v7x, 256 devices: a whole 4x4x8 slice. The times are simulated.
256 devices in a mesh: seq: 32 (over z, x_hi, core), fsdp: 8 (over x_lo, y).
Axes of the slice: x: 4 (x_hi: 2, x_lo: 2; x = x_hi * 2 + x_lo), y: 4, z: 8, core: 2. Of those that a mesh axis runs over, the one named last changes fastest.
Arguments:
- text_states: bfloat16 [8192, 8192], P('seq'), may hold values from -6 to 6
- images: bfloat16 [32, 1601, 8192], P('seq', None, 'fsdp'), may hold values from -6 to 6
- norm_gain: float32 [8192], replicated, may hold values from 0.1 to 1.9
- query_weight: bfloat16 [8192, 4096], P('seq', 'fsdp'), may hold values from -0.0625 to 0.0625
- image_projection_weight: bfloat16 [8192, 2048], P(('fsdp', 'seq')), may hold values from -0.0625 to 0.0625
- query_gain: float32 [128], replicated, may hold values from 0.5 to 2
- key_gain: float32 [128], replicated, may hold values from 0.5 to 2
- admission: int32 [32, 32], P('seq'), may hold values from 0 to 1, as said below
Outputs:
- attended: bfloat16 [8192, 4096], P('seq', 'fsdp')
Inputs may be any that keep to these rules, and one draw needn't show every extreme that they name: admission[c, m] is 1 for m = c and for at most 2 of the images m with c - 4 <= m < c, and 0 elsewhere; in every draw some text blocks, the last one among them, attend to exactly 3 images.
All inputs are finite; a program needn't handle non-finite values.
Results may differ from a plain program's by a relative error of at most 0.035.
Values may be sent and summed in bfloat16 or wider, within the bound.
No kernel may reach another device: no remote copies, remote signals or barrier semaphores. Data moves between devices by JAX's collectives and lax.ppermute only.
A program may use at most 128 MiB of HBM per device.

v0:
```python
import math
import jax
import jax.numpy as jnp
from jax import lax
from jax.sharding import PartitionSpec as P

KEY_VALUE_HEADS = 8
IMAGE_LOOKBACK = 4


def from_behind(value, axis, steps):
    count = lax.axis_size(axis)
    initial, last = (max(0, -steps), min(count, count - steps))
    return lax.ppermute(value, axis, [(source, source + steps) for source in range(initial, last)])


def rms_scale(values, gain):
    return values * lax.rsqrt(jnp.mean(values * values, axis=-1, keepdims=True) + 1e-05) * gain


def attend(query_heads, stacked, admitted):
    slot_count, kv_heads, image_tokens, double_width = stacked.shape
    head_dim = double_width // 2
    row_count, heads_local, _ = query_heads.shape
    heads_per_group = heads_local // kv_heads
    grouped = query_heads.reshape(row_count, kv_heads, heads_per_group, head_dim)
    grouped = grouped.transpose(1, 2, 0, 3).reshape(kv_heads, heads_per_group * row_count, head_dim)
    per_head = jnp.moveaxis(stacked, 1, 0).reshape(
        kv_heads, slot_count * image_tokens, double_width
    )
    column_live = jnp.repeat(admitted, image_tokens)
    score_scale = 1.0 / math.sqrt(head_dim)

    def one_head(operands):
        query_rows, key_value_pair = operands
        scores = (
            lax.dot_general(
                query_rows,
                key_value_pair[:, :head_dim],
                (((1,), (1,)), ((), ())),
                preferred_element_type=jnp.float32,
            )
            * score_scale
        )
        scores = jnp.where(column_live[None, :], scores, -jnp.inf)
        row_peak = jnp.max(scores, axis=1, keepdims=True)
        weights = jnp.exp(scores - row_peak)
        row_total = jnp.sum(weights, axis=1, keepdims=True)
        blended = jnp.dot(
            weights.astype(jnp.bfloat16),
            key_value_pair[:, head_dim:],
            preferred_element_type=jnp.float32,
        )
        return blended / row_total

    outputs = lax.map(one_head, (grouped, per_head))
    outputs = outputs.reshape(kv_heads, heads_per_group, row_count, head_dim).transpose(2, 0, 1, 3)
    return outputs.reshape(row_count, heads_local * head_dim).astype(jnp.bfloat16)


def on_device(
    text_states,
    images,
    norm_gain,
    query_weight,
    image_projection_weight,
    query_gain,
    key_gain,
    admission,
):
    head_dim = query_gain.shape[0]
    local_key_value = KEY_VALUE_HEADS // lax.axis_size("fsdp")
    heads_local = query_weight.shape[1] // head_dim
    row_count = text_states.shape[0]
    normed = rms_scale(text_states.astype(jnp.float32), norm_gain).astype(jnp.bfloat16)
    columns = normed
    queries = jnp.dot(
        columns,
        lax.all_gather(query_weight, "seq", axis=0, tiled=True),
        preferred_element_type=jnp.float32,
    )
    query_heads = rms_scale(queries.reshape(row_count, heads_local, head_dim), query_gain).astype(
        jnp.bfloat16
    )
    weight_block = lax.all_gather(image_projection_weight, "seq", axis=0, tiled=True)
    features = images[0]
    columns = weight_block
    score_product = jnp.dot(features, columns, preferred_element_type=jnp.float32)
    own_kv = lax.psum_scatter(
        score_product.reshape(
            features.shape[0], local_key_value * lax.axis_size("fsdp"), 2 * head_dim
        )
        .transpose(1, 0, 2)
        .astype(jnp.bfloat16),
        "fsdp",
        scatter_dimension=0,
        tiled=True,
    ).astype(jnp.float32)
    key_part = rms_scale(own_kv[..., :head_dim], key_gain)
    packed = jnp.concatenate([key_part, own_kv[..., head_dim:]], axis=-1).astype(jnp.bfloat16)
    image_window = [packed]
    for distance in range(1, IMAGE_LOOKBACK + 1):
        image_window.append(from_behind(packed, "seq", distance))
    stacked = jnp.stack(image_window)
    span_index = lax.axis_index("seq")
    image_ids = span_index - jnp.arange(IMAGE_LOOKBACK + 1, dtype=jnp.int32)
    admitted = (image_ids >= 0) & (jnp.take(admission[0], jnp.maximum(image_ids, 0)) == 1)
    return attend(query_heads, stacked, admitted)


def solution(mesh):
    placed = (
        P("seq", None),
        P("seq", None, "fsdp"),
        P(),
        P("seq", "fsdp"),
        P(("fsdp", "seq"), None),
        P(),
        P(),
        P("seq", None),
    )
    return jax.shard_map(
        on_device, mesh=mesh, in_specs=placed, out_specs=P("seq", "fsdp"), check_vma=False
    )
```

profile of v0, /device:TPU:129, one launch (start us, length us, event | category | flops | bytes accessed | tf_op | source)
XLA Modules:
  0.0 410.5 jit_solution(13469132266472897213)
XLA Ops:
  6.5 0.7 all-gather.5.cloned.1.call-update
  7.3 0.0 all-gather.3.cloned.1.call-start
  7.3 0.7 all-gather.3.cloned.1.call-update
  8.0 0.0 reduce-scatter.2.cloned.1.call-start
  8.1 88.1 %all-gather.5.cloned.1.call-done = bf16[1024,2048]{1,0:T(8,128)(2,1)} async-done(((bf16[32,2048]{1,0:T(8,128)(2,1)}), bf16[1024,2048]{1,0:T(8,128)(2,1)}) %all-gather.5.cloned.1.call-update) | async-done | bytes 4194320 | tf_op jit(solution)/shard_map/all_gather | solution.py:85
  96.1 6.4 %copy.20 = bf16[2048,1024]{1,0:T(8,128)(2,1)} copy(bf16[2048,1024]{0,1:T(8,128)(2,1)} %bitcast.39) | data formatting | bytes 8388608 | tf_op jit(solution)/shard_map/dot_general | solution.py:88
  102.5 11.0 %convert_bitcast_fusion = bf16[8,1601,256]{2,1,0:T(8,128)(2,1)} fusion(bf16[8,256,1024]{2,1,0:T(8,128)(2,1)} %bitcast.40, bf16[1,1601,1024]{2,1,0:T(8,128)(2,1)S(1)} %copy-done), kind=kOutput, calls=%fused_computation.13 | convolution fusion | flops 6718359552 | bytes 14030848 | tf_op jit(solution)/shard_map/dot_general | solution.py:88
  113.5 0.0 reduce-scatter.2.cloned.1.call-update
  113.6 0.6 copy-done.2
  114.2 0.6 gather_fusion
  114.8 0.1 broadcast_in_dim.37
  114.9 0.1 broadcast_in_dim.38
  115.0 3.1 fusion.6
  118.1 78.7 %all-gather.3.cloned.1.call-done = bf16[8192,512]{1,0:T(8,128)(2,1)} async-done(((bf16[256,512]{1,0:T(8,128)(2,1)}), bf16[8192,512]{1,0:T(8,128)(2,1)}) %all-gather.3.cloned.1.call-update) | async-done | bytes 8388624 | tf_op jit(solution)/shard_map/all_gather | solution.py:79
  196.8 7.0 %fusion.31 = (f32[256,512]{1,0:T(8,128)S(1)}, f32[256,512]{1,0:T(8,128)S(1)}) fusion(bf16[8192,512]{1,0:T(8,128)(2,1)} %all-gather.3.cloned.1.call-done, bf16[256,8192]{1,0:T(8,128)(2,1)} %param.8, f32[8192]{0:T(1024)S(1)} %copy-done.7, f32[256]{0:T(256)S(1)} %add_rsqrt_fusion.2), kind=kOutput, calls=%fused_computation.45 | convolution fusion | flops 2156003328 | bytes 13665280 | tf_op jit(solution)/shard_map/dot_general | solution.py:77
  203.9 0.0 copy-start.5
  203.9 0.2 mul.84
  204.1 0.3 reduce_sum.38
  204.4 0.1 copy.18
  204.5 0.2 reshape.144
  204.7 0.2 fusion.28
  204.9 72.2 %reduce-scatter.2.cloned.1.call-done = bf16[1,1601,256]{2,1,0:T(8,128)(2,1)} async-done(((bf16[8,1601,256]{2,1,0:T(8,128)(2,1)}), bf16[1,1601,256]{2,1,0:T(8,128)(2,1)}) %reduce-scatter.2.cloned.1.call-update) | async-done | bytes 819728 | tf_op jit(solution)/shard_map/reduce_scatter | solution.py:89
  277.1 1.4 convert_element_type.62
  278.5 0.3 multiply_reduce_fusion
  278.9 0.0 copy-done.5
  278.9 0.3 multiply_convert_fusion
  279.2 0.1 pad_maximum_fusion
  279.3 4.8 %collective-permute-start = (bf16[1,1601,256]{2,1,0:T(8,128)(2,1)S(1)}, bf16[1,1601,256]{2,1,0:T(8,128)(2,1)S(1)}, u32[]{:S(2)}, u32[]{:S(2)}) collective-permute-start(bf16[1,1601,256]{2,1,0:T(8,128)(2,1)S(1)} %pad_maximum_fusion), channel_id=1, source_target_pairs={{0,8},{8,16},{16,24},{24,32},{32,40},{40,48},{48,56},{56,64},{64,7... | collective-permute-start | bytes 2459144 | tf_op jit(solution)/shard_map/ppermute | solution.py:14
  284.1 0.3 fusion.35
  284.4 2.3 collective-permute-start.3
  286.7 1.9 collective-permute-start.2
  288.6 2.7 collective-permute-start.1
  291.4 1.0 maximum_dynamic-update-slice_fusion
  292.4 4.1 collective-permute-done
  296.5 1.0 bitcast_dynamic-update-slice_fusion.3
  297.4 52.0 %collective-permute-done.1 = bf16[1,1601,256]{2,1,0:T(8,128)(2,1)S(1)} collective-permute-done((bf16[1,1601,256]{2,1,0:T(8,128)(2,1)S(1)}, bf16[1,1601,256]{2,1,0:T(8,128)(2,1)S(1)}, u32[]{:S(2)}, u32[]{:S(2)}) %collective-permute-start.1) | collective-permute-done | bytes 819744 | tf_op jit(solution)/shard_map/ppermute | solution.py:14
  349.5 1.0 bitcast_dynamic-update-slice_fusion.2
  350.4 0.0 collective-permute-done.2
  350.4 1.0 bitcast_dynamic-update-slice_fusion.1
  351.4 0.0 collective-permute-done.3
  351.4 1.0 bitcast_dynamic-update-slice_fusion
  352.3 5.2 %squeeze.19 = bf16[8005,256]{1,0:T(8,128)(2,1)} reshape(bf16[5,1,1601,256]{3,2,1,0:T(8,128)(2,1)} %bitcast_dynamic-update-slice_fusion) | data formatting | bytes 8197120 | tf_op jit(solution)/shard_map/while/body/jit(dynamic_index_in_dim)/squeeze | solution.py:56
  357.5 13.8 %fusion = (f32[1024]{0:T(1024)S(1)}, f32[1024,8005]{0,1:T(8,128)}) fusion(pred[8005]{0:T(1024)(128)(4,1)S(1)} %broadcast_in_dim.38, bf16[1024,128]{1,0:T(8,128)(2,1)S(1)} %bitcast.41, bf16[8005,256]{1,0:T(8,128)(2,1)} %squeeze.19), kind=kOutput, calls=%fused_computation.3 | convolution fusion | flops 2123053056 | bytes 35112772 | tf_op jit(solution)/shard_map/while/body/eval_jaxpr/dot_general | solution.py:37
  371.4 15.1 %fusion.1 = f32[1024]{0:T(1024)S(1)} fusion(f32[1024,8005]{0,1:T(8,128)} %get-tuple-element.22, f32[1024]{0:T(1024)S(1)} %get-tuple-element.20, pred[8005]{0:T(1024)(128)(4,1)S(1)} %broadcast_in_dim.38), kind=kLoop, calls=%fused_computation.4 | loop fusion | flops 32787456 | bytes 32804676 | tf_op jit(solution)/shard_map/while/body/eval_jaxpr/reduce_sum | solution.py:48
  386.4 0.0 copy-start.1
  386.5 16.6 %fusion.22 = bf16[1024,128]{1,0:T(8,128)(2,1)S(1)} fusion(bf16[8005,256]{1,0:T(8,128)(2,1)S(1)} %copy-done.3, f32[1024,8005]{0,1:T(8,128)} %get-tuple-element.22, f32[1024]{0:T(1024)S(1)} %get-tuple-element.20, pred[8005]{0:T(1024)(128)(4,1)S(1)} %broadcast_in_dim.38, f32[1024]{0:T(1024)S(1)} %fusion.1), kind=kOutput, calls=%fused_computation.22 | convolution fusion | flops 2131513344 | bytes 35117056 | tf_op jit(solution)/shard_map/while/body/eval_jaxpr/dot_general | solution.py:49
  403.0 0.2 copy.21
  403.3 0.7 copy.29
  (22 shorter events, 0.1 us)
Async XLA Ops:
  6.5 96.0 %copy-start = (bf16[1,1601,1024]{2,1,0:T(8,128)(2,1)S(1)}, bf16[1,1601,1024]{2,1,0:T(8,128)(2,1)}, u32[]{:S(2)}) copy-start(bf16[1,1601,1024]{2,1,0:T(8,128)(2,1)} %param.9) | copy-start | bytes 9836548
  6.5 89.6 %all-gather.5.cloned.1.call-start = ((), (), s32[]{:S(2)}) async-start(), calls=%async_computation.2 | async-start | bytes 4325376 | tf_op jit(solution)/shard_map/all_gather | solution.py:85
  7.3 189.5 %all-gather.3.cloned.1.call-start = ((), (), s32[]{:S(2)}) async-start(), calls=%async_computation.1 | async-start | bytes 8650752 | tf_op jit(solution)/shard_map/all_gather | solution.py:79
  8.0 269.1 %reduce-scatter.2.cloned.1.call-start = ((), (), s32[]{:S(2)}) async-start(), calls=%async_computation.3 | async-start | bytes 7409664 | tf_op jit(solution)/shard_map/reduce_scatter | solution.py:89
  113.5 0.7 copy-start.2
  113.5 83.3 %copy-start.7 = (f32[8192]{0:T(1024)S(1)}, f32[8192]{0:T(1024)}, u32[]{:S(2)}) copy-start(f32[8192]{0:T(1024)} %param.10) | copy-start | bytes 98308
  118.1 86.6 %copy-start.6 = (f32[128]{0:T(128)S(1)}, f32[128]{0:T(128)}, u32[]{:S(2)}) copy-start(f32[128]{0:T(128)} %param.13) | copy-start | bytes 1540
  203.9 75.0 %copy-start.5 = (f32[128]{0:T(128)S(1)}, f32[128]{0:T(128)}, u32[]{:S(2)}) copy-start(f32[128]{0:T(128)} %param.14) | copy-start | bytes 1540
  277.1 2.0 slice-start
  277.1 14.2 %copy-start.4 = (bf16[1,1601,256]{2,1,0:T(8,128)(2,1)S(1)}, bf16[1,1601,256]{2,1,0:T(8,128)(2,1)}, u32[]{:S(2)}) copy-start(bf16[1,1601,256]{2,1,0:T(8,128)(2,1)} %reduce-scatter.2.cloned.1.call-done) | copy-start | bytes 2459140
  279.3 17.2 %collective-permute-start = (bf16[1,1601,256]{2,1,0:T(8,128)(2,1)S(1)}, bf16[1,1601,256]{2,1,0:T(8,128)(2,1)S(1)}, u32[]{:S(2)}, u32[]{:S(2)}) collective-permute-start(bf16[1,1601,256]{2,1,0:T(8,128)(2,1)S(1)} %pad_maximum_fusion), channel_id=1, source_target_pairs={{0,8},{8,16},{16,24},{24,32},{32,40},{40,48},{48,56},{56,64},{64,7... | collective-permute-start | bytes 2459144 | tf_op jit(solution)/shard_map/ppermute | solution.py:14
  284.4 67.0 %collective-permute-start.3 = (bf16[1,1601,256]{2,1,0:T(8,128)(2,1)S(1)}, bf16[1,1601,256]{2,1,0:T(8,128)(2,1)S(1)}, u32[]{:S(2)}, u32[]{:S(2)}) collective-permute-start(bf16[1,1601,256]{2,1,0:T(8,128)(2,1)S(1)} %pad_maximum_fusion), channel_id=1, source_target_pairs={{0,32},{8,40},{16,48},{24,56},{32,64},{40,72},{48,80},{56,88},{64,... | collective-permute-start | bytes 2459144 | tf_op jit(solution)/shard_map/ppermute | solution.py:14
  286.7 63.7 %collective-permute-start.2 = (bf16[1,1601,256]{2,1,0:T(8,128)(2,1)S(1)}, bf16[1,1601,256]{2,1,0:T(8,128)(2,1)S(1)}, u32[]{:S(2)}, u32[]{:S(2)}) collective-permute-start(bf16[1,1601,256]{2,1,0:T(8,128)(2,1)S(1)} %pad_maximum_fusion), channel_id=1, source_target_pairs={{0,24},{8,32},{16,40},{24,48},{32,56},{40,64},{48,72},{56,80},{64,... | collective-permute-start | bytes 2459144 | tf_op jit(solution)/shard_map/ppermute | solution.py:14
  288.6 60.8 %collective-permute-start.1 = (bf16[1,1601,256]{2,1,0:T(8,128)(2,1)S(1)}, bf16[1,1601,256]{2,1,0:T(8,128)(2,1)S(1)}, u32[]{:S(2)}, u32[]{:S(2)}) collective-permute-start(bf16[1,1601,256]{2,1,0:T(8,128)(2,1)S(1)} %pad_maximum_fusion), channel_id=1, source_target_pairs={{0,16},{8,24},{16,32},{24,40},{32,48},{40,56},{48,64},{56,72},{64,... | collective-permute-start | bytes 2459144 | tf_op jit(solution)/shard_map/ppermute | solution.py:14
  371.4 15.1 %copy-start.3 = (bf16[8005,256]{1,0:T(8,128)(2,1)S(1)}, bf16[8005,256]{1,0:T(8,128)(2,1)}, u32[]{:S(2)}) copy-start(bf16[8005,256]{1,0:T(8,128)(2,1)} %squeeze.19) | copy-start | bytes 12295684
  386.4 17.6 %copy-start.1 = (bf16[1,1601,1024]{2,1,0:T(8,128)(2,1)S(1)}, bf16[1,1601,1024]{2,1,0:T(8,128)(2,1)}, u32[]{:S(2)}) copy-start(bf16[1,1601,1024]{2,1,0:T(8,128)(2,1)} %param.9) | copy-start | bytes 9836548
Sparse Core Ops, SparseCore 0:
  10.1 85.9 all-gather.4
  98.9 97.8 all-gather.2
  199.4 77.6 reduce-scatter.1
where the time goes:
time: 411 us
  waiting for transfers between devices  296 us (72%)
  matrix products  48.4 us (12%)
  other arithmetic  22.1 us (5%)
  local copies, waits for them, and re-layouts  18.3 us (4%)
  between operations  13.4 us (3%)
  starting transfers between devices  11.9 us (3%)
    all_gather x1, waiting for transfers between devices, on_device(): lax.all_gather(image_projection_weight, 'seq', axis=0, tiled=True)  88.1 us
    all_gather x1, waiting for transfers between devices, on_device(): lax.all_gather(query_weight, 'seq', axis=0, tiled=True)  78.7 us
    reduce_scatter x1, waiting for transfers between devices, on_device(): lax.psum_scatter(score_product.reshape(features.shape[0], local_key_value...  72.2 us
    ppermute x4, waiting for transfers between devices, from_behind(): lax.ppermute(value, axis, [(source, source + steps) for source in range(i...  56.1 us
    dot_general x1, matrix products, one_head(): jnp.dot(weights.astype(jnp.bfloat16), key_value_pair[:, head_dim:], prefe...  16.6 us
    reduce_sum x1, other arithmetic, one_head(): row_total = jnp.sum(weights, axis=1, keepdims=True)  15.1 us
    dot_general x1, matrix products, one_head(): lax.dot_general(query_rows, key_value_pair[:, :head_dim], (((1,), (1,)),...  13.8 us
    ppermute x4, starting transfers between devices, from_behind(): lax.ppermute(value, axis, [(source, source + steps) for source in range(i...  11.8 us
  transfers between devices with their start and end apart: 7, of which 5 were waited for; matrix products, arithmetic and copies ran while one was open for 8% of the time, Pallas kernels for 0%

commit v1 on v0

--- a/solution.py
+++ b/solution.py
@@ -3,6 +3,7 @@
 import jax.numpy as jnp
 from jax import lax
 from jax.sharding import PartitionSpec as P
+from jax.lax import all_to_all, psum
 
 KEY_VALUE_HEADS = 8
 IMAGE_LOOKBACK = 4
@@ -68,6 +69,15 @@
     key_gain,
     admission,
 ):
+
+    def threads_use(block_in, chip_axis):
+        nodes = []
+        for _ in range(psum(1, axis_name=chip_axis)):
+            nodes.append(block_in)
+        return jnp.concatenate(
+            all_to_all(jnp.stack(nodes), chip_axis, concat_axis=0, split_axis=0), axis=0
+        )
+
     head_dim = query_gain.shape[0]
     local_key_value = KEY_VALUE_HEADS // lax.axis_size("fsdp")
     heads_local = query_weight.shape[1] // head_dim
@@ -82,7 +92,7 @@
     query_heads = rms_scale(queries.reshape(row_count, heads_local, head_dim), query_gain).astype(
         jnp.bfloat16
     )
-    weight_block = lax.all_gather(image_projection_weight, "seq", axis=0, tiled=True)
+    weight_block = threads_use(image_projection_weight, "seq")
     features = images[0]
     columns = weight_block
     score_product = jnp.dot(features, columns, preferred_element_type=jnp.float32)

time: 411 us -> 365 us (0.89)
  waiting for transfers between devices: 296 us -> 123 us
  blocking collectives: 0 us -> 123 us
    all_to_all x0 -> x1, blocking collectives: none -> 123 us  [threads_use(): all_to_all(jnp.stack(nodes), chip_axis, concat_axis=0, split_axis=0)]
    all_gather x1 -> x0, waiting for transfers between devices: 88.1 us -> none  [on_device(): lax.all_gather(image_projection_weight, 'seq', axis=0, tiled=True)]
    all_gather x1, waiting for transfers between devices: 78.7 us -> 0.02 us  [on_device(): lax.all_gather(query_weight, 'seq', axis=0, tiled=True)]
    reduce_scatter x1, waiting for transfers between devices: 72.2 us -> 66.5 us  [on_device(): lax.psum_scatter(score_product.reshape(features.shape[0], local_key_value...]
  transfers between devices with their start and end apart: 7 -> 6, of which waited for: 5 -> 3; matrix products, arithmetic and copies ran while one was open for 8% -> 10% of each run, Pallas kernels for 0% -> 0%
where the time goes in v1:
time: 365 us; the launch traced here: 364 us
  waiting for transfers between devices  123 us (34%)
  blocking collectives  123 us (34%)
  matrix products  48.6 us (13%)
  other arithmetic  22.1 us (6%)
  local copies, waits for them, and re-layouts  19.9 us (5%)
  between operations  15.1 us (4%)
  starting transfers between devices  11.9 us (3%)
    all_to_all x1, blocking collectives, threads_use(): all_to_all(jnp.stack(nodes), chip_axis, concat_axis=0, split_axis=0)  123 us
    reduce_scatter x1, waiting for transfers between devices, on_device(): lax.psum_scatter(score_product.reshape(features.shape[0], local_key_value...  66.5 us
    ppermute x4, waiting for transfers between devices, from_behind(): lax.ppermute(value, axis, [(source, source + steps) for source in range(i...  56.1 us
    dot_general x1, matrix products, one_head(): jnp.dot(weights.astype(jnp.bfloat16), key_value_pair[:, head_dim:], prefe...  16.6 us
    reduce_sum x1, other arithmetic, one_head(): row_total = jnp.sum(weights, axis=1, keepdims=True)  15.1 us
    dot_general x1, matrix products, one_head(): lax.dot_general(query_rows, key_value_pair[:, :head_dim], (((1,), (1,)),...  13.8 us
    ppermute x4, starting transfers between devices, from_behind(): lax.ppermute(value, axis, [(source, source + steps) for source in range(i...  11.9 us
    dot_general x1, matrix products, on_device(): jnp.dot(features, columns, preferred_element_type=jnp.float32)  11.2 us
  transfers between devices with their start and end apart: 6, of which 3 were waited for; matrix products, arithmetic and copies ran while one was open for 10% of the time, Pallas kernels for 0%

profile of v1, /device:TPU:129, one launch (start us, length us, event | category | flops | bytes accessed | tf_op | source)
XLA Modules:
  0.0 363.8 jit_solution(11948679769578988679)
XLA Ops:
  7.4 0.7 all-gather.2.cloned.1.call-update
  8.1 0.0 reduce-scatter.2.cloned.1.call-start
  8.1 1.6 stack.12
  9.8 122.8 %all_to_all.5 = bf16[32,32,2048]{2,1,0:T(8,128)(2,1)} all-to-all(bf16[32,32,2048]{2,1,0:T(8,128)(2,1)S(1)} %stack.12), channel_id=1, replica_groups=mesh['seq'=32,'fsdp'=8] {'seq'}, dimensions={0} | all-to-all | bytes 8388608 | tf_op jit(solution)/shard_map/all_to_all | solution.py:78
  132.6 6.4 %copy.20 = bf16[2048,1024]{1,0:T(8,128)(2,1)} copy(bf16[2048,1024]{0,1:T(8,128)(2,1)} %bitcast.41) | data formatting | bytes 8388608 | tf_op jit(solution)/shard_map/dot_general | solution.py:98
  139.0 11.2 %convert_bitcast_fusion = bf16[8,1601,256]{2,1,0:T(8,128)(2,1)} fusion(bf16[8,256,1024]{2,1,0:T(8,128)(2,1)} %bitcast.42, bf16[1,1601,1024]{2,1,0:T(8,128)(2,1)S(1)} %copy-done), kind=kOutput, calls=%fused_computation.13 | convolution fusion | flops 6718359552 | bytes 14030848 | tf_op jit(solution)/shard_map/dot_general | solution.py:98
  150.2 0.0 reduce-scatter.2.cloned.1.call-update
  150.2 0.6 copy-done.2
  150.8 0.6 gather_fusion
  151.5 0.1 broadcast_in_dim.37
  151.6 0.1 broadcast_in_dim.38
  151.7 3.1 fusion.6
  154.8 0.0 all-gather.2.cloned.1.call-done
  154.9 7.0 %fusion.31 = (f32[256,512]{1,0:T(8,128)S(1)}, f32[256,512]{1,0:T(8,128)S(1)}) fusion(bf16[8192,512]{1,0:T(8,128)(2,1)} %all-gather.2.cloned.1.call-done, bf16[256,8192]{1,0:T(8,128)(2,1)} %param.8, f32[8192]{0:T(1024)S(1)} %copy-done.7, f32[256]{0:T(256)S(1)} %add_rsqrt_fusion.2), kind=kOutput, calls=%fused_computation.45 | convolution fusion | flops 2156003328 | bytes 13665280 | tf_op jit(solution)/shard_map/dot_general | solution.py:87
  161.9 0.0 copy-start.5
  161.9 0.2 mul.84
  162.1 0.3 reduce_sum.38
  162.4 0.1 copy.18
  162.5 0.2 reshape.149
  162.7 0.0 copy-done.6
  162.7 0.2 fusion.28
  163.0 66.5 %reduce-scatter.2.cloned.1.call-done = bf16[1,1601,256]{2,1,0:T(8,128)(2,1)} async-done(((bf16[8,1601,256]{2,1,0:T(8,128)(2,1)}), bf16[1,1601,256]{2,1,0:T(8,128)(2,1)}) %reduce-scatter.2.cloned.1.call-update) | async-done | bytes 819728 | tf_op jit(solution)/shard_map/reduce_scatter | solution.py:99
  229.4 1.4 convert_element_type.62
  230.8 0.3 multiply_reduce_fusion
  231.2 0.3 multiply_convert_fusion
  231.4 0.0 slice-done
  231.5 0.1 pad_maximum_fusion
  231.6 4.9 %collective-permute-start = (bf16[1,1601,256]{2,1,0:T(8,128)(2,1)S(1)}, bf16[1,1601,256]{2,1,0:T(8,128)(2,1)S(1)}, u32[]{:S(2)}, u32[]{:S(2)}) collective-permute-start(bf16[1,1601,256]{2,1,0:T(8,128)(2,1)S(1)} %pad_maximum_fusion), channel_id=1, source_target_pairs={{0,8},{8,16},{16,24},{24,32},{32,40},{40,48},{48,56},{56,64},{64,7... | collective-permute-start | bytes 2459144 | tf_op jit(solution)/shard_map/ppermute | solution.py:15
  236.5 0.3 fusion.35
  236.8 2.3 collective-permute-start.3
  239.1 1.9 collective-permute-start.2
  241.0 2.8 collective-permute-start.1
  243.8 1.0 maximum_dynamic-update-slice_fusion
  244.8 4.0 %collective-permute-done = bf16[1,1601,256]{2,1,0:T(8,128)(2,1)S(1)} collective-permute-done((bf16[1,1601,256]{2,1,0:T(8,128)(2,1)S(1)}, bf16[1,1601,256]{2,1,0:T(8,128)(2,1)S(1)}, u32[]{:S(2)}, u32[]{:S(2)}) %collective-permute-start) | collective-permute-done | bytes 819744 | tf_op jit(solution)/shard_map/ppermute | solution.py:15
  248.8 1.0 bitcast_dynamic-update-slice_fusion.3
  249.8 52.0 %collective-permute-done.1 = bf16[1,1601,256]{2,1,0:T(8,128)(2,1)S(1)} collective-permute-done((bf16[1,1601,256]{2,1,0:T(8,128)(2,1)S(1)}, bf16[1,1601,256]{2,1,0:T(8,128)(2,1)S(1)}, u32[]{:S(2)}, u32[]{:S(2)}) %collective-permute-start.1) | collective-permute-done | bytes 819744 | tf_op jit(solution)/shard_map/ppermute | solution.py:15
  301.8 0.9 bitcast_dynamic-update-slice_fusion.2
  302.8 0.0 collective-permute-done.2
  302.8 0.9 bitcast_dynamic-update-slice_fusion.1
  303.7 0.0 collective-permute-done.3
  303.7 1.0 bitcast_dynamic-update-slice_fusion
  304.7 5.2 %squeeze.19 = bf16[8005,256]{1,0:T(8,128)(2,1)} reshape(bf16[5,1,1601,256]{3,2,1,0:T(8,128)(2,1)} %bitcast_dynamic-update-slice_fusion) | data formatting | bytes 8197120 | tf_op jit(solution)/shard_map/while/body/jit(dynamic_index_in_dim)/squeeze | solution.py:57
  309.9 13.8 %fusion = (f32[1024]{0:T(1024)S(1)}, f32[1024,8005]{0,1:T(8,128)}) fusion(pred[8005]{0:T(1024)(128)(4,1)S(1)} %broadcast_in_dim.38, bf16[1024,128]{1,0:T(8,128)(2,1)S(1)} %bitcast.43, bf16[8005,256]{1,0:T(8,128)(2,1)} %squeeze.19), kind=kOutput, calls=%fused_computation.3 | convolution fusion | flops 2123053056 | bytes 35112772 | tf_op jit(solution)/shard_map/while/body/eval_jaxpr/dot_general | solution.py:38
  323.7 15.1 %fusion.1 = f32[1024]{0:T(1024)S(1)} fusion(f32[1024,8005]{0,1:T(8,128)} %get-tuple-element.22, f32[1024]{0:T(1024)S(1)} %get-tuple-element.20, pred[8005]{0:T(1024)(128)(4,1)S(1)} %broadcast_in_dim.38), kind=kLoop, calls=%fused_computation.4 | loop fusion | flops 32787456 | bytes 32804676 | tf_op jit(solution)/shard_map/while/body/eval_jaxpr/reduce_sum | solution.py:49
  338.8 0.0 copy-start.1
  338.8 16.6 %fusion.22 = bf16[1024,128]{1,0:T(8,128)(2,1)S(1)} fusion(bf16[8005,256]{1,0:T(8,128)(2,1)S(1)} %copy-done.3, f32[1024,8005]{0,1:T(8,128)} %get-tuple-element.22, f32[1024]{0:T(1024)S(1)} %get-tuple-element.20, pred[8005]{0:T(1024)(128)(4,1)S(1)} %broadcast_in_dim.38, f32[1024]{0:T(1024)S(1)} %fusion.1), kind=kOutput, calls=%fused_computation.22 | convolution fusion | flops 2131513344 | bytes 35117056 | tf_op jit(solution)/shard_map/while/body/eval_jaxpr/dot_general | solution.py:50
  355.4 0.2 copy.21
  355.6 0.7 copy.29
  (21 shorter events, 0.1 us)
Async XLA Ops:
  7.4 131.7 %copy-start = (bf16[1,1601,1024]{2,1,0:T(8,128)(2,1)S(1)}, bf16[1,1601,1024]{2,1,0:T(8,128)(2,1)}, u32[]{:S(2)}) copy-start(bf16[1,1601,1024]{2,1,0:T(8,128)(2,1)} %param.9) | copy-start | bytes 9836548
  7.4 147.5 %all-gather.2.cloned.1.call-start = ((), (), s32[]{:S(2)}) async-start(), calls=%async_computation.2 | async-start | bytes 8650752 | tf_op jit(solution)/shard_map/all_gather | solution.py:89
  8.1 221.3 %reduce-scatter.2.cloned.1.call-start = ((), (), s32[]{:S(2)}) async-start(), calls=%async_computation.3 | async-start | bytes 7409664 | tf_op jit(solution)/shard_map/reduce_scatter | solution.py:99
  150.2 0.7 copy-start.2
  150.2 4.7 %copy-start.7 = (f32[8192]{0:T(1024)S(1)}, f32[8192]{0:T(1024)}, u32[]{:S(2)}) copy-start(f32[8192]{0:T(1024)} %param.10) | copy-start | bytes 98308
  154.8 7.9 %copy-start.6 = (f32[128]{0:T(128)S(1)}, f32[128]{0:T(128)}, u32[]{:S(2)}) copy-start(f32[128]{0:T(128)} %param.13) | copy-start | bytes 1540
  161.9 69.3 %copy-start.5 = (f32[128]{0:T(128)S(1)}, f32[128]{0:T(128)}, u32[]{:S(2)}) copy-start(f32[128]{0:T(128)} %param.14) | copy-start | bytes 1540
  229.4 2.0 slice-start
  229.4 14.3 %copy-start.4 = (bf16[1,1601,256]{2,1,0:T(8,128)(2,1)S(1)}, bf16[1,1601,256]{2,1,0:T(8,128)(2,1)}, u32[]{:S(2)}) copy-start(bf16[1,1601,256]{2,1,0:T(8,128)(2,1)} %reduce-scatter.2.cloned.1.call-done) | copy-start | bytes 2459140
  231.6 17.3 %collective-permute-start = (bf16[1,1601,256]{2,1,0:T(8,128)(2,1)S(1)}, bf16[1,1601,256]{2,1,0:T(8,128)(2,1)S(1)}, u32[]{:S(2)}, u32[]{:S(2)}) collective-permute-start(bf16[1,1601,256]{2,1,0:T(8,128)(2,1)S(1)} %pad_maximum_fusion), channel_id=1, source_target_pairs={{0,8},{8,16},{16,24},{24,32},{32,40},{40,48},{48,56},{56,64},{64,7... | collective-permute-start | bytes 2459144 | tf_op jit(solution)/shard_map/ppermute | solution.py:15
  236.8 67.0 %collective-permute-start.3 = (bf16[1,1601,256]{2,1,0:T(8,128)(2,1)S(1)}, bf16[1,1601,256]{2,1,0:T(8,128)(2,1)S(1)}, u32[]{:S(2)}, u32[]{:S(2)}) collective-permute-start(bf16[1,1601,256]{2,1,0:T(8,128)(2,1)S(1)} %pad_maximum_fusion), channel_id=1, source_target_pairs={{0,32},{8,40},{16,48},{24,56},{32,64},{40,72},{48,80},{56,88},{64,... | collective-permute-start | bytes 2459144 | tf_op jit(solution)/shard_map/ppermute | solution.py:15
  239.1 63.7 %collective-permute-start.2 = (bf16[1,1601,256]{2,1,0:T(8,128)(2,1)S(1)}, bf16[1,1601,256]{2,1,0:T(8,128)(2,1)S(1)}, u32[]{:S(2)}, u32[]{:S(2)}) collective-permute-start(bf16[1,1601,256]{2,1,0:T(8,128)(2,1)S(1)} %pad_maximum_fusion), channel_id=1, source_target_pairs={{0,24},{8,32},{16,40},{24,48},{32,56},{40,64},{48,72},{56,80},{64,... | collective-permute-start | bytes 2459144 | tf_op jit(solution)/shard_map/ppermute | solution.py:15
  241.0 60.9 %collective-permute-start.1 = (bf16[1,1601,256]{2,1,0:T(8,128)(2,1)S(1)}, bf16[1,1601,256]{2,1,0:T(8,128)(2,1)S(1)}, u32[]{:S(2)}, u32[]{:S(2)}) collective-permute-start(bf16[1,1601,256]{2,1,0:T(8,128)(2,1)S(1)} %pad_maximum_fusion), channel_id=1, source_target_pairs={{0,16},{8,24},{16,32},{24,40},{32,48},{40,56},{48,64},{56,72},{64,... | collective-permute-start | bytes 2459144 | tf_op jit(solution)/shard_map/ppermute | solution.py:15
  323.7 15.1 %copy-start.3 = (bf16[8005,256]{1,0:T(8,128)(2,1)S(1)}, bf16[8005,256]{1,0:T(8,128)(2,1)}, u32[]{:S(2)}) copy-start(bf16[8005,256]{1,0:T(8,128)(2,1)} %squeeze.19) | copy-start | bytes 12295684
  338.8 17.6 %copy-start.1 = (bf16[1,1601,1024]{2,1,0:T(8,128)(2,1)S(1)}, bf16[1,1601,1024]{2,1,0:T(8,128)(2,1)}, u32[]{:S(2)}) copy-start(bf16[1,1601,1024]{2,1,0:T(8,128)(2,1)} %param.9) | copy-start | bytes 9836548
Sparse Core Ops, SparseCore 0:
  11.4 135.1 all-gather.1
Sparse Core Ops, SparseCore 1:
  150.3 79.0 reduce-scatter.1
